TPU v7x, 128 devices: a whole 4x4x4 slice. The times are simulated.
128 devices in a mesh: valve: 8 (over y, core), bulk: 16 (over z, x).
Axes of the slice: x: 4, y: 4, z: 4, core: 2. Of those that a mesh axis runs over, the one named last changes fastest.
Arguments:
- solution: float32 [5, 64, 131072], P(None, None, ('valve', 'bulk')), may hold values from -6 to 6
- velocity: float32 [3, 131072], P(None, ('valve', 'bulk')), may hold values from -1 to 1
- inv_jacobian: float32 [64, 131072], P(None, ('valve', 'bulk')), may hold values from 0.5 to 3
- face_speed: float32 [96, 131072], P(None, ('valve', 'bulk')), may hold values from -6 to 6
- face_link: int32 [6, 131072], P(None, ('valve', 'bulk')), may hold values from 0 to 6271, as said below
- donor_elem: int32 [1048576], P(('valve', 'bulk')), may hold values from 0 to 1023
- ref_coords: float32 [3, 1048576], P(None, ('valve', 'bulk')), may hold values from -1 to 1
- owner_list: int32 [1048576, 1], P(('valve', 'bulk')), may hold values from 0 to 15; in each aligned block of 8192 rows (0 to 8191, 8192 to 16383, ...) at most 1024 rows name the same one
Outputs:
- section_rate: float32 [5, 64, 131072], P(None, None, ('valve', 'bulk'))
- fringe_values: float32 [5, 2097152], P(None, ('valve', 'bulk'))
Inputs may be any that keep to these rules, and one draw needn't show every extreme that they name: `face_link`: on each device, the values 6 * 1024 to 6271 appear exactly once each; every other face slot links to another slot of the same device that links back to it. `owner_list`: among the receptors of one device no owner is named more than 1024 times; in every draw some device names some owner exactly 1024 times.
All inputs are finite; a program needn't handle non-finite values.
Results may differ from a plain program's by a relative error of at most 0.0003.
Values sent between devices are 32-bit elements; how exact they have to be, the bound alone decides.
No kernel may reach another device: no remote copies, remote signals or barrier semaphores. Data moves between devices by JAX's collectives and lax.ppermute only.
A program may use at most 192 MiB of HBM per device.

v0:
```python
import jax
import jax.numpy as jnp
import numpy as np
from jax import lax
from jax.sharding import PartitionSpec as P

gauss_nodes = (-0.8611363115940526, -0.3399810435848563, 0.3399810435848563, 0.8611363115940526)
quad_weights = (0.3478548451374538, 0.6521451548625461, 0.6521451548625461, 0.3478548451374538)
section_step = 0.2


def padded(shard, sides, width):
    for axis, dim in sides:
        size, length = (lax.axis_size(axis), shard.shape[dim])
        up = [(i, (i + 1) % size) for i in range(size)]
        down = [(j, i) for i, j in up]
        last = lax.slice_in_dim(shard, length - width, length, axis=dim)
        initial = lax.slice_in_dim(shard, 0, width, axis=dim)
        before = lax.ppermute(last, axis, up)
        after = lax.ppermute(initial, axis, down)
        shard = jnp.concatenate([before, shard, after], axis=dim)
    return shard


def lagrange_at(x):
    values = []
    for j in range(4):
        factor = 1.0
        for m in range(4):
            if m != j:
                factor = factor * (x - gauss_nodes[m]) / (gauss_nodes[j] - gauss_nodes[m])
        values.append(factor)
    return values


def tables():
    slopes = np.zeros((4, 4))
    for i in range(4):
        for j in range(4):
            summed = 0.0
            for m in range(4):
                if m != j:
                    product = 1.0 / (gauss_nodes[j] - gauss_nodes[m])
                    for n in range(4):
                        if n != j and n != m:
                            product = (
                                product
                                * (gauss_nodes[i] - gauss_nodes[n])
                                / (gauss_nodes[j] - gauss_nodes[n])
                            )
                    summed = summed + product
            slopes[i, j] = summed
    end_values = [lagrange_at(-1.0), lagrange_at(1.0)]
    extrapolate = np.zeros((96, 64))
    lifting = np.zeros((64, 96))
    derivative = np.zeros((3, 64, 64))
    for p in range(64):
        point_idx = (p // 16, p // 4 % 4, p % 4)
        for f in range(6):
            normal_dir = f // 2
            across = [t for t in range(3) if t != normal_dir]
            q = point_idx[across[0]] * 4 + point_idx[across[1]]
            flux_row = q * 6 + f
            extrapolate[flux_row, p] = end_values[f % 2][point_idx[normal_dir]]
            lifting[p, flux_row] = (
                end_values[f % 2][point_idx[normal_dir]] / quad_weights[point_idx[normal_dir]]
            )
        for s in range(64):
            other_idx = (s // 16, s // 4 % 4, s % 4)
            for normal_dir in range(3):
                if all((point_idx[t] == other_idx[t] for t in range(3) if t != normal_dir)):
                    derivative[normal_dir, p, s] = slopes[
                        point_idx[normal_dir], other_idx[normal_dir]
                    ]
    return (
        jnp.asarray(extrapolate, dtype=jnp.float32),
        jnp.asarray(derivative, dtype=jnp.float32),
        jnp.asarray(lifting, dtype=jnp.float32),
    )


def face_rows(solution, face_speed, extrapolate):
    nvars = solution.shape[0]
    elems = solution.shape[2]
    ext_faces = extrapolate.reshape(16, 6, 64)
    values = jnp.einsum("qfp,vpe->feqv", ext_faces, solution, precision=lax.Precision.HIGHEST)
    values = values.reshape(6 * elems, 16, nvars)
    speeds = jnp.transpose(face_speed.reshape(16, 6, elems), (1, 2, 0)).reshape(6 * elems, 16)
    return (values, speeds)


def rim_rows(table_own, links, faces_total, rim_count):
    slots = jnp.where(links >= faces_total, links - faces_total, 2 * rim_count)
    senders = (
        jnp.zeros((2 * rim_count,), jnp.int32)
        .at[slots]
        .set(jnp.arange(faces_total, dtype=jnp.int32), mode="drop")
    )
    return jnp.take(table_own, senders, axis=0)


def surface_term(values, speeds, table_own, links, received, lifting, elems):
    nvars = values.shape[2]
    full_table = jnp.concatenate([table_own, received], axis=0)
    outer = jnp.take(full_table, links, axis=0)
    outer_vals = outer[:, : 16 * nvars].reshape(6 * elems, 16, nvars)
    outer_speed = outer[:, 16 * nvars :][:, :, None]
    own_speed = speeds[:, :, None]
    normal = 0.5 * (own_speed - outer_speed)
    common = 0.5 * normal * (values + outer_vals) + 0.5 * jnp.abs(normal) * (values - outer_vals)
    jump_term = (common - own_speed * values).reshape(6, elems, 16, nvars)
    lift_faces = lifting.reshape(64, 16, 6)
    return jnp.einsum("pqf,feqv->vpe", lift_faces, jump_term, precision=lax.Precision.HIGHEST)


def volume_term(solution, velocity, derivative):
    slopes = jnp.einsum("dpq,vqe->dvpe", derivative, solution, precision=lax.Precision.HIGHEST)
    return jnp.sum(velocity[:, None, None, :] * slopes, axis=0)


def receptor_rows(advanced, donors, coords):
    nvars = advanced.shape[0]
    elems = advanced.shape[2]
    basis_x = jnp.stack(lagrange_at(coords[0]))
    basis_y = jnp.stack(lagrange_at(coords[1]))
    basis_z = jnp.stack(lagrange_at(coords[2]))
    weights = (
        basis_x[:, None, None, :] * basis_y[None, :, None, :] * basis_z[None, None, :, :]
    ).reshape(64, -1)
    element_rows = jnp.transpose(advanced, (2, 0, 1)).reshape(elems, nvars * 64)
    picked = jnp.take(element_rows, donors, axis=0).reshape(donors.shape[0], nvars, 64)
    return jnp.einsum("rvp,pr->rv", picked, weights, precision=lax.Precision.HIGHEST)


def on_device(
    solution, velocity, inv_jacobian, face_speed, face_link, donor_elem, ref_coords, owner_list
):
    extrapolate, derivative, lifting = tables()
    nvars = solution.shape[0]
    elems = solution.shape[2]
    rim_count = elems // 16
    faces_total = 6 * elems
    links = face_link.reshape(faces_total)
    values, speeds = face_rows(solution, face_speed, extrapolate)
    table_own = jnp.concatenate([values.reshape(faces_total, 16 * nvars), speeds], axis=1)
    outgoing = rim_rows(table_own, links, faces_total, rim_count)
    extended = padded(outgoing, (("valve", 0),), rim_count)
    received = jnp.concatenate([extended[:rim_count], extended[3 * rim_count :]], axis=0)
    surface = surface_term(values, speeds, table_own, links, received, lifting, elems)
    volume = volume_term(solution, velocity, derivative)
    section_rate = -inv_jacobian[None] * (volume + surface)
    advanced = solution + section_step * section_rate
    receptor_vals = receptor_rows(advanced, donor_elem, ref_coords)
    buckets = lax.axis_size("bulk")
    receptors = receptor_vals.shape[0]
    capacity = 2 * receptors // buckets
    owners = owner_list[:, 0]
    gathered_vals, gathered_owners = (
        lax.all_gather(receptor_vals, "bulk", axis=0, tiled=True),
        lax.all_gather(owners, "bulk", axis=0, tiled=True),
    )
    by_source = gathered_owners.reshape(buckets, receptors)
    matches = (by_source == lax.axis_index("bulk")).astype(jnp.int32)
    before = jnp.cumsum(matches, axis=1) - matches
    places = jnp.where(
        matches == 1,
        jnp.arange(buckets, dtype=jnp.int32)[:, None] * capacity + before,
        buckets * capacity,
    ).reshape(buckets * receptors)
    fringe_rows = jnp.zeros((buckets * capacity, nvars), jnp.float32)
    fringe_rows = fringe_rows.at[places].set(gathered_vals, mode="drop")
    return (section_rate, jnp.transpose(fringe_rows))


def solution(mesh):
    placed = (
        P(None, None, ("valve", "bulk")),
        P(None, ("valve", "bulk")),
        P(None, ("valve", "bulk")),
        P(None, ("valve", "bulk")),
        P(None, ("valve", "bulk")),
        P(("valve", "bulk")),
        P(None, ("valve", "bulk")),
        P(("valve", "bulk"), None),
    )
    return jax.shard_map(
        on_device,
        mesh=mesh,
        in_specs=placed,
        out_specs=(P(None, None, ("valve", "bulk")), P(None, ("valve", "bulk"))),
        check_vma=False,
    )
```

profile of v0, /device:TPU:1, one launch (start us, length us, event | category | flops | bytes accessed | tf_op | source)
XLA Modules:
  0.0 905.8 jit_solution(7143843174503303031)
XLA Ops:
  8.1 23.0 %scatter_custom_fusion = s32[128]{0:T(128)S(1)} fusion(s32[6144]{0:T(1024)S(1)} %bitcast.87, s32[6144]{0:T(1024)S(1)} %iota.8, s32[]{:T(128)} %constant.125.clone.1), kind=kCustom, calls=%fused_computation.82 | custom fusion | bytes 516 | tf_op jit(solution)/shard_map/scatter | solution.py:97
  31.1 1.8 reshape.165
  33.0 1.9 copy.19
  34.9 4.0 convolution_bitcast_fusion
  38.9 1.2 copy.20
  40.1 2.5 copy.44
  42.6 3.4 copy.21
  46.1 4.6 pad_maximum_fusion.1
  50.6 2.6 gather_fusion
  53.3 2.7 collective-permute-start
  58.0 4.4 multiply_reduce_fusion.1
  63.0 22.0 %all-gather = s32[131072,1]{0,1:T(1,128)} all-gather(s32[8192,1]{0,1:T(1,128)S(1)} %copy-done.16), channel_id=2, replica_groups=mesh['valve'=8,'bulk'=16] {'bulk'}, dimensions={0}, use_global_device_ids=true | all-gather | bytes 557056 | tf_op jit(solution)/shard_map/all_gather | solution.py:160
  86.0 2.0 mul.255
  88.6 3.8 pad_maximum_fusion
  92.3 21.1 %gather_fusion.1 = f32[6144,96]{1,0:T(8,128)} fusion(f32[6272,96]{1,0:T(8,128)S(1)} %pad_maximum_fusion, s32[6144]{0:T(1024)S(1)} %broadcast_clamp_fusion), kind=kCustom, calls=%fused_computation.1 | custom fusion | bytes 4743168 | tf_op jit(solution)/shard_map/jit(_take)/gather | solution.py:105
  113.4 4.8 broadcast_select_fusion
  118.2 3.5 broadcast_multiply_fusion
  121.7 2.2 copy.23
  123.8 3.4 reshape.169
  127.2 3.2 copy.22
  130.4 3.0 copy.25
  133.4 7.4 multiply_add_fusion
  140.8 1.8 copy.29
  142.6 34.8 %gather_fusion.2 = f32[8192,320]{1,0:T(8,128)} fusion(f32[1024,320]{1,0:T(8,128)S(1)} %copy.29, s32[8192]{0:T(1024)} %fusion.25), kind=kCustom, calls=%fused_computation.2 | custom fusion | bytes 21004288 | tf_op jit(solution)/shard_map/jit(_take)/gather | solution.py:131
  177.5 12.1 %copy.30 = f32[8192,320]{0,1:T(8,128)} copy(f32[8192,320]{1,0:T(8,128)} %gather_fusion.2) | data formatting | bytes 20971520 | tf_op jit(solution)/shard_map/jit(_take)/gather | solution.py:131
  189.5 5.7 multiply_reduce_fusion
  195.2 2.7 copy.42
  197.9 1.0 copy-done.8
  199.6 5.0 reduce-window.6
  205.7 365.4 %all-gather.3.cloned.1.call-done = f32[131072,5]{1,0:T(8,128)} async-done(((f32[8192,5]{1,0:T(8,128)}), f32[131072,5]{1,0:T(8,128)}) %all-gather.3.cloned.1.call-update) | async-done | bytes 2621456 | tf_op jit(solution)/shard_map/all_gather | solution.py:159
  571.1 321.9 %scatter_custom_fusion.1 = f32[16384,5]{1,0:T(8,128)} fusion(s32[131072]{0:T(1024)S(1)} %compare_select_fusion, f32[131072,5]{1,0:T(8,128)} %all-gather.3.cloned.1.call-done, f32[]{:T(128)} %constant.124.clone.1), kind=kCustom, calls=%fused_computation.6 | custom fusion | bytes 328192 | tf_op jit(solution)/shard_map/scatter | solution.py:171
  893.0 6.0 copy.31
  (68 shorter events, 6.9 us)
Async XLA Ops:
  7.2 27.7 %copy-start.14 = (f32[16,6,64,1]{2,0,3,1:T(8,128)S(1)}, f32[16,6,64,1]{2,0,3,1:T(8,128)}, u32[]{:S(2)}) copy-start(f32[16,6,64,1]{2,0,3,1:T(8,128)} %constant.160) | copy-start | bytes 73732
  7.2 563.9 %all-gather.3.cloned.1.call-start = ((), (), s32[]{:S(2)}) async-start(), calls=%async_computation | async-start | bytes 71303168 | tf_op jit(solution)/shard_map/all_gather | solution.py:159
  34.9 11.1 %copy-start = (f32[6,1024,16]{2,1,0:T(8,128)}, f32[6,1024,16]{2,1,0:T(8,128)S(1)}, u32[]{:S(2)}) copy-start(f32[6,1024,16]{2,1,0:T(8,128)S(1)} %copy.19) | copy-start | bytes 1179652
  38.9 3.7 copy-start.2
  46.0 10.0 %copy-start.10 = (s32[6,1024]{1,0:T(8,128)S(1)}, s32[6,1024]{1,0:T(8,128)}, u32[]{:S(2)}) copy-start(s32[6,1024]{1,0:T(8,128)} %param.15) | copy-start | bytes 73732
  46.0 10.0 %copy-start.11 = (s32[8192]{0:T(1024)S(1)}, s32[8192]{0:T(1024)}, u32[]{:S(2)}) copy-start(s32[8192]{0:T(1024)} %param.16) | copy-start | bytes 98308
  46.0 10.7 %copy-start.13 = (f32[3,8192]{1,0:T(4,128)S(1)}, f32[3,8192]{1,0:T(4,128)}, u32[]{:S(2)}) copy-start(f32[3,8192]{1,0:T(4,128)} %param.17) | copy-start | bytes 294916
  46.0 11.9 %copy-start.12 = (f32[3,64,64,1]{2,1,3,0:T(8,128)S(1)}, f32[3,64,64,1]{2,1,3,0:T(8,128)}, u32[]{:S(2)}) copy-start(f32[3,64,64,1]{2,1,3,0:T(8,128)} %constant.159) | copy-start | bytes 147460
  46.0 11.9 %copy-start.17 = (f32[3,1024]{1,0:T(4,128)S(1)}, f32[3,1024]{1,0:T(4,128)}, u32[]{:S(2)}) copy-start(f32[3,1024]{1,0:T(4,128)} %param.12) | copy-start | bytes 36868
  50.6 7.3 copy-start.4
  53.3 34.6 %collective-permute-start = (f32[64,96]{1,0:T(8,128)S(1)}, f32[64,96]{1,0:T(8,128)S(1)}, u32[]{:S(2)}, u32[]{:S(2)}) collective-permute-start(f32[64,96]{1,0:T(8,128)S(1)} %get-tuple-element.18), channel_id=1, source_target_pairs={{0,16},{16,32},{32,48},{48,64},{64,80},{80,96},{96,112},{112,0},{1... | collective-permute-start | bytes 73736 | tf_op jit(solution)/shard_map/ppermute | solution.py:19
  56.0 32.5 %collective-permute-start.1 = (f32[64,96]{1,0:T(8,128)S(1)}, f32[64,96]{1,0:T(8,128)}, u32[]{:S(2)}, u32[]{:S(2)}) collective-permute-start(f32[64,96]{1,0:T(8,128)S(1)} %get-tuple-element.19), channel_id=1, source_target_pairs={{16,0},{32,16},{48,32},{64,48},{80,64},{96,80},{112,96},{0,112},{1... | collective-permute-start | bytes 73736 | tf_op jit(solution)/shard_map/ppermute | solution.py:20
  57.8 5.2 copy-start.16
  57.9 27.1 %copy-start.7 = (f32[16,6,1024]{2,1,0:T(8,128)S(1)}, f32[16,6,1024]{2,1,0:T(8,128)}, u32[]{:S(2)}) copy-start(f32[16,6,1024]{2,1,0:T(8,128)} %reshape.165) | copy-start | bytes 1179652
  57.9 28.0 %copy-start.9 = (f32[64,1024]{1,0:T(8,128)S(1)}, f32[64,1024]{1,0:T(8,128)}, u32[]{:S(2)}) copy-start(f32[64,1024]{1,0:T(8,128)} %param.13) | copy-start | bytes 786436
  88.0 0.6 copy-start.15
  113.4 4.8 copy-start.1
  127.2 6.2 copy-start.3
  127.2 6.2 copy-start.5
  177.5 12.1 %copy-start.6 = (f32[64,8192]{1,0:T(8,128)S(1)}, f32[64,8192]{1,0:T(8,128)}, u32[]{:S(2)}) copy-start(f32[64,8192]{1,0:T(8,128)} %mul.255) | copy-start | bytes 6291460
  197.9 1.0 copy-start.8
Sparse Core Ops, SparseCore 0:
  198.1 372.9 all-gather.2
where the time goes:
time: 907 us; the launch traced here: 906 us
  local copies, waits for them, and re-layouts  455 us (50%)
  waiting for transfers between devices  365 us (40%)
  other arithmetic  30.8 us (3%)
  blocking collectives  22 us (2%)
  matrix products  15.8 us (2%)
  between operations  14.4 us (2%)
    all_gather x1, waiting for transfers between devices, on_device(): lax.all_gather(receptor_vals, 'bulk', axis=0, tiled=True)  365 us
    scatter x1, local copies, waits for them, and re-layouts, on_device(): fringe_rows = fringe_rows.at[places].set(gathered_vals, mode='drop')  322 us
    gather x2, local copies, waits for them, and re-layouts, receptor_rows(): jnp.take(element_rows, donors, axis=0).reshape(donors.shape[0], nvars, 64)  46.9 us
    scatter x1, local copies, waits for them, and re-layouts, rim_rows(): senders = jnp.zeros((2 * rim_count,), jnp.int32).at[slots].set(jnp.arange...  23 us
    all_gather x1, blocking collectives, on_device(): lax.all_gather(owners, 'bulk', axis=0, tiled=True)  22 us
    gather x1, local copies, waits for them, and re-layouts, surface_term(): outer = jnp.take(full_table, links, axis=0)  21.1 us
  transfers between devices with their start and end apart: 3, of which 1 were waited for; matrix products, arithmetic and copies ran while one was open for 2% of the time, Pallas kernels for 0%

commit v1 on v0

--- a/solution.py
+++ b/solution.py
@@ -156,7 +156,9 @@
     capacity = 2 * receptors // buckets
     owners = owner_list[:, 0]
     gathered_vals, gathered_owners = (
-        lax.all_gather(receptor_vals, "bulk", axis=0, tiled=True),
+        jnp.concatenate(
+            lax.all_to_all(jnp.stack([receptor_vals] * lax.axis_size("bulk")), "bulk", 0, 0), axis=0
+        ),
         lax.all_gather(owners, "bulk", axis=0, tiled=True),
     )
     by_source = gathered_owners.reshape(buckets, receptors)

time: 907 us -> 620 us (0.68); the launches traced: 906 us -> 610 us
  waiting for transfers between devices: 365 us -> 46.1 us
  local copies, waits for them, and re-layouts: 455 us -> 486 us
  between operations: 14.4 us -> 1.01 us
    all_gather x1 -> x0, waiting for transfers between devices: 365 us -> none  [on_device(): lax.all_gather(receptor_vals, 'bulk', axis=0, tiled=True)]
    all_to_all x0 -> x1, waiting for transfers between devices: none -> 46.1 us  [on_device(): lax.all_to_all(jnp.stack([receptor_vals] * lax.axis_size('bulk')), 'bulk'...]
    reshape x0 -> x1, local copies, waits for them, and re-layouts: none -> 30.4 us  [on_device(): jnp.concatenate(lax.all_to_all(jnp.stack([receptor_vals] * lax.axis_size(...]
  transfers between devices with their start and end apart: 3 -> 3, of which waited for: 1 -> 1; matrix products, arithmetic and copies ran while one was open for 2% -> 3% of each run, Pallas kernels for 0% -> 0%
where the time goes in v1:
time: 620 us; the launch traced here: 610 us
  local copies, waits for them, and re-layouts  486 us (78%)
  waiting for transfers between devices  46.1 us (7%)
  other arithmetic  32.1 us (5%)
  blocking collectives  20.4 us (3%)
  matrix products  16.6 us (3%)
  starting transfers between devices  7.6 us (1%)
    scatter x1, local copies, waits for them, and re-layouts, on_device(): fringe_rows = fringe_rows.at[places].set(gathered_vals, mode='drop')  322 us
    gather x2, local copies, waits for them, and re-layouts, receptor_rows(): jnp.take(element_rows, donors, axis=0).reshape(donors.shape[0], nvars, 64)  46.9 us
    all_to_all x1, waiting for transfers between devices, on_device(): lax.all_to_all(jnp.stack([receptor_vals] * lax.axis_size('bulk')), 'bulk'...  46.1 us
    reshape x1, local copies, waits for them, and re-layouts, on_device(): jnp.concatenate(lax.all_to_all(jnp.stack([receptor_vals] * lax.axis_size(...  30.4 us
    scatter x1, local copies, waits for them, and re-layouts, rim_rows(): senders = jnp.zeros((2 * rim_count,), jnp.int32).at[slots].set(jnp.arange...  23 us
    gather x1, local copies, waits for them, and re-layouts, surface_term(): outer = jnp.take(full_table, links, axis=0)  21.1 us
    all_gather x1, blocking collectives, on_device(): lax.all_gather(owners, 'bulk', axis=0, tiled=True)  20.4 us
  transfers between devices with their start and end apart: 3, of which 1 were waited for; matrix products, arithmetic and copies ran while one was open for 3% of the time, Pallas kernels for 0%

profile of v1, /device:TPU:1, one launch (start us, length us, event | category | flops | bytes accessed | tf_op | source)
XLA Modules:
  0.0 609.7 jit_solution(16229186019303480778)
XLA Ops:
  1.5 23.0 %scatter_custom_fusion = s32[128]{0:T(128)S(1)} fusion(s32[6144]{0:T(1024)S(1)} %bitcast.88, s32[6144]{0:T(1024)S(1)} %iota.8, s32[]{:T(128)} %constant.125.clone.1), kind=kCustom, calls=%fused_computation.82 | custom fusion | bytes 516 | tf_op jit(solution)/shard_map/scatter | solution.py:97
  24.5 1.8 reshape.170
  26.4 1.9 copy.44
  28.3 4.0 convolution_bitcast_fusion
  33.5 2.5 copy.67
  36.1 3.4 copy.46
  39.4 4.5 pad_maximum_fusion.1
  44.0 2.5 gather_fusion
  47.2 2.7 collective-permute-start
  52.3 20.4 %all-gather = s32[131072,1]{0,1:T(1,128)S(1)} all-gather(s32[8192,1]{0,1:T(1,128)S(1)} %copy-done.20), channel_id=2, replica_groups=mesh['valve'=8,'bulk'=16] {'bulk'}, dimensions={0}, use_global_device_ids=true | all-gather | bytes 557056 | tf_op jit(solution)/shard_map/all_gather | solution.py:162
  74.0 4.8 reduce-window.6
  81.7 5.2 multiply_reduce_fusion.1
  89.5 1.7 mul.255
  91.2 3.8 pad_maximum_fusion
  95.0 21.1 %gather_fusion.1 = f32[6144,96]{1,0:T(8,128)} fusion(f32[6272,96]{1,0:T(8,128)S(1)} %pad_maximum_fusion, s32[6144]{0:T(1024)S(1)} %broadcast_clamp_fusion), kind=kCustom, calls=%fused_computation.1 | custom fusion | bytes 4743168 | tf_op jit(solution)/shard_map/jit(_take)/gather | solution.py:105
  116.0 4.8 broadcast_select_fusion
  120.9 3.5 broadcast_multiply_fusion
  124.3 2.2 copy.48
  126.5 3.4 reshape.174
  129.9 3.1 copy.47
  133.0 3.0 copy.50
  136.1 7.4 %multiply_add_fusion = (f32[5,64,1024]{2,1,0:T(8,128)}, f32[5,64,1024]{2,1,0:T(8,128)}) fusion(f32[5,64,1024]{2,1,0:T(8,128)S(1)} %copy-done.5, f32[64,16,6,1]{0,1,3,2:T(8,128)} %constant.161, f32[6,1024,16,5]{1,2,3,0:T(8,128)S(1)} %copy-done.3, f32[6,1024,16,5]{1,0,3,2:T(8,128)} %reshape.174, f32[6,1024,16]{1,2,0:T(8,128)} %copy.52, ...), kind=kOutput, calls=%fused_computation.32 | convolution fusion | flops 382238720 | bytes 10641408 | tf_op jit(solution)/shard_map/pqf,feqv->vpe/dot_general | solution.py:113
  143.5 1.8 copy.53
  145.3 34.9 %gather_fusion.2 = f32[8192,320]{1,0:T(8,128)} fusion(f32[1024,320]{1,0:T(8,128)S(1)} %copy.53, s32[8192]{0:T(1024)} %fusion.25), kind=kCustom, calls=%fused_computation.2 | custom fusion | bytes 21004288 | tf_op jit(solution)/shard_map/jit(_take)/gather | solution.py:131
  180.1 12.1 %copy.54 = f32[8192,320]{0,1:T(8,128)} copy(f32[8192,320]{1,0:T(8,128)} %gather_fusion.2) | data formatting | bytes 20971520 | tf_op jit(solution)/shard_map/jit(_take)/gather | solution.py:131
  192.2 5.7 multiply_reduce_fusion
  197.9 2.4 stack.11
  200.3 4.9 all-to-all-start
  205.3 46.1 %all-to-all-done = f32[16,8192,5]{1,2,0:T(8,128)} async-done(((f32[16,8192,5]{1,2,0:T(8,128)}), f32[16,8192,5]{1,2,0:T(8,128)}, u32[]{:S(2)}, u32[]{:S(2)}) %all-to-all-start) | async-done | bytes 2621472 | tf_op jit(solution)/shard_map/all_to_all | solution.py:160
  251.5 30.4 %copy.55 = f32[131072,5]{1,0:T(8,128)} copy(f32[131072,5]{0,1:T(8,128)} %bitcast.25) | data formatting | bytes 5242880 | tf_op jit(solution)/shard_map/reshape | solution.py:159
  281.9 321.9 %scatter_custom_fusion.1 = f32[16384,5]{1,0:T(8,128)} fusion(s32[131072]{0:T(1024)S(1)} %compare_select_fusion, f32[131072,5]{1,0:T(8,128)} %copy.55, f32[]{:T(128)} %constant.124.clone.1), kind=kCustom, calls=%fused_computation.6 | custom fusion | bytes 328192 | tf_op jit(solution)/shard_map/scatter | solution.py:173
  603.7 6.0 copy.56
  (74 shorter events, 12.0 us)
Async XLA Ops:
  0.6 27.7 %copy-start.19 = (f32[16,6,64,1]{2,0,3,1:T(8,128)S(1)}, f32[16,6,64,1]{2,0,3,1:T(8,128)}, u32[]{:S(2)}) copy-start(f32[16,6,64,1]{2,0,3,1:T(8,128)} %constant.160) | copy-start | bytes 73732
  28.3 11.1 %copy-start = (f32[6,1024,16]{2,1,0:T(8,128)}, f32[6,1024,16]{2,1,0:T(8,128)S(1)}, u32[]{:S(2)}) copy-start(f32[6,1024,16]{2,1,0:T(8,128)S(1)} %copy.44) | copy-start | bytes 1179652
  32.3 3.7 copy-start.2
  39.4 10.5 %copy-start.15 = (s32[6,1024]{1,0:T(8,128)S(1)}, s32[6,1024]{1,0:T(8,128)}, u32[]{:S(2)}) copy-start(s32[6,1024]{1,0:T(8,128)} %param.15) | copy-start | bytes 73732
  39.4 10.5 %copy-start.16 = (s32[8192]{0:T(1024)S(1)}, s32[8192]{0:T(1024)}, u32[]{:S(2)}) copy-start(s32[8192]{0:T(1024)} %param.16) | copy-start | bytes 98308
  39.4 11.2 %copy-start.18 = (f32[3,8192]{1,0:T(4,128)S(1)}, f32[3,8192]{1,0:T(4,128)}, u32[]{:S(2)}) copy-start(f32[3,8192]{1,0:T(4,128)} %param.17) | copy-start | bytes 294916
  39.4 12.9 %copy-start.20 = (s32[8192,1]{0,1:T(1,128)S(1)}, s32[8192,1]{0,1:T(1,128)}, u32[]{:S(2)}) copy-start(s32[8192,1]{0,1:T(1,128)} %param.18) | copy-start | bytes 98308
  47.2 44.0 %collective-permute-start = (f32[64,96]{1,0:T(8,128)}, f32[64,96]{1,0:T(8,128)}, u32[]{:S(2)}, u32[]{:S(2)}) collective-permute-start(f32[64,96]{1,0:T(8,128)} %get-tuple-element.22), channel_id=1, source_target_pairs={{0,16},{16,32},{32,48},{48,64},{64,80},{80,96},{96,112},{112,0},{1... | collective-permute-start | bytes 73736 | tf_op jit(solution)/shard_map/ppermute | solution.py:19
  49.9 41.3 %collective-permute-start.1 = (f32[64,96]{1,0:T(8,128)}, f32[64,96]{1,0:T(8,128)}, u32[]{:S(2)}, u32[]{:S(2)}) collective-permute-start(f32[64,96]{1,0:T(8,128)} %get-tuple-element.23), channel_id=1, source_target_pairs={{16,0},{32,16},{48,32},{64,48},{80,64},{96,80},{112,96},{0,112},{1... | collective-permute-start | bytes 73736 | tf_op jit(solution)/shard_map/ppermute | solution.py:20
  73.2 0.8 copy-start.8
  78.8 2.9 copy-start.4
  78.8 2.9 copy-start.17
  80.8 6.0 copy-start.7
  81.1 6.8 %copy-start.14 = (f32[64,1024]{1,0:T(8,128)S(1)}, f32[64,1024]{1,0:T(8,128)}, u32[]{:S(2)}) copy-start(f32[64,1024]{1,0:T(8,128)} %param.13) | copy-start | bytes 786436
  81.1 7.5 %copy-start.10 = (s32[2,64,8,128]{3,2,1,0:T(8,128)S(1)}, s32[2,64,8,128]{3,2,1,0:T(8,128)}, u32[]{:S(2)}) copy-start(s32[2,64,8,128]{3,2,1,0:T(8,128)} %broadcast_bitcast_fusion) | copy-start | bytes 1572868
  116.0 4.8 copy-start.1
  129.9 6.2 %copy-start.3 = (f32[6,1024,16,5]{1,2,3,0:T(8,128)S(1)}, f32[6,1024,16,5]{1,2,3,0:T(8,128)}, u32[]{:S(2)}) copy-start(f32[6,1024,16,5]{1,2,3,0:T(8,128)} %copy-done.2) | copy-start | bytes 5898244
  129.9 6.2 %copy-start.5 = (f32[5,64,1024]{2,1,0:T(8,128)S(1)}, f32[5,64,1024]{2,1,0:T(8,128)}, u32[]{:S(2)}) copy-start(f32[5,64,1024]{2,1,0:T(8,128)} %param.11) | copy-start | bytes 3932164
  129.9 6.2 %copy-start.13 = (f32[64,1024]{1,0:T(8,128)S(1)}, f32[64,1024]{1,0:T(8,128)}, u32[]{:S(2)}) copy-start(f32[64,1024]{1,0:T(8,128)} %neg.4) | copy-start | bytes 786436
  180.1 12.1 %copy-start.6 = (f32[64,8192]{1,0:T(8,128)S(1)}, f32[64,8192]{1,0:T(8,128)}, u32[]{:S(2)}) copy-start(f32[64,8192]{1,0:T(8,128)} %mul.255) | copy-start | bytes 6291460
  200.2 4.9 copy-start.9
  200.2 4.9 copy-start.11
  200.3 5.0 copy-start.12
  200.3 51.2 %all-to-all-start = ((f32[16,8192,5]{1,2,0:T(8,128)}), f32[16,8192,5]{1,2,0:T(8,128)}, u32[]{:S(2)}, u32[]{:S(2)}) async-start(f32[16,8192,5]{1,2,0:T(8,128)} %stack.11), calls=%async_computation | async-start | bytes 8388608 | tf_op jit(solution)/shard_map/all_to_all | solution.py:160
